TPU v7x, 32 devices: a whole 2x2x4 slice. The times are simulated.
32 devices in a mesh: dp: 8 (over y, x, core), fsdp: 4 (over z).
Axes of the slice: x: 2, y: 2, z: 4, core: 2. Of those that a mesh axis runs over, the one named last changes fastest.
Arguments:
- activations: bfloat16 [8192, 4096], P(('dp', 'fsdp')), may hold values from -8 to 8
- cotangents: bfloat16 [8192, 4096], P('dp', 'fsdp'), may hold values from -8 to 8
- group_ids: int32 [32, 256], P(('dp', 'fsdp')), may hold values from 0 to 7, as said below
- weights: float32 [4096, 4096], P('fsdp', 'dp'), may hold values from -0.09375 to 0.09375
- first_moment: float32 [4096, 4096], P('fsdp', 'dp'), may hold values from -3 to 3
- second_moment: float32 [4096, 4096], P('fsdp', 'dp'), may hold values from 0.01 to 0.1
- fresh_noise: bfloat16 [4096, 4096], P('fsdp', 'dp'), may hold values from -6 to 6
- history: bfloat16 [16, 4096, 4096], P('dp', 'fsdp'), may hold values from -6 to 6
- slot_ids: int32 [16], P('dp'), may hold values from 0 to 15, each once
- band_coefs: float32 [16], replicated, may hold values from 0.3 to 1
- step_number: int32 [1], replicated, may hold values from 16 to 99999
- noise_mult: float32 [1], replicated, may hold values from 0.002 to 0.008
Outputs:
- new_weights: float32 [4096, 4096], P('fsdp', 'dp')
- new_first: float32 [4096, 4096], P('fsdp', 'dp')
- new_second: float32 [4096, 4096], P('fsdp', 'dp')
- noisy_mean: float32 [4096, 4096], P('fsdp', 'dp')
- gathered_weights: float32 [4096, 4096], P('fsdp')
- new_history: bfloat16 [16, 4096, 4096], P('dp', 'fsdp')
Inputs may be any that keep to these rules, and one draw needn't show every extreme that they name: `group_ids`: in each row the ids never fall; each of the 8 ids names 1 to 64 tokens, one of them exactly 64. `slot_ids`: each cycle position is held by exactly one entry.
All inputs are finite; a program needn't handle non-finite values.
Results may differ from a plain program's by a relative error of at most 0.002.
Values may be sent and summed in bfloat16 or wider, within the bound.
No kernel may reach another device: no remote copies, remote signals or barrier semaphores. Data moves between devices by JAX's collectives and lax.ppermute only.
A program may use at most 192 MiB of HBM per device.

v0:
```python
import jax
import jax.numpy as jnp
from jax import lax
from jax.sharding import PartitionSpec as P

D_IN = 4096
D_OUT = 4096
BAND = 16
GROUP_MOST = 64
EX_DEV = 8


def clip_bound():
    return ((GROUP_MOST * GROUP_MOST / 4.0 + GROUP_MOST) * D_IN * D_OUT) ** 0.5


def body(
    activations,
    cotangents,
    group_ids,
    weights,
    first_moment,
    second_moment,
    fresh_noise,
    history,
    slot_ids,
    band_coefs,
    step_number,
    noise_mult,
):
    clip = clip_bound()
    token_count = activations.shape[0]
    out_local = cotangents.shape[1]
    step_value = step_number[0]
    target = step_value % BAND
    full_fresh = lax.all_gather(fresh_noise, "dp", axis=1, tiled=True)
    new_history = jnp.where((slot_ids == target)[:, None, None], full_fresh[None], history)
    blocks = cotangents.reshape(cotangents.shape[0] // token_count, token_count, out_local)
    partial_gram = jnp.einsum("ati,asi->ats", blocks, blocks, preferred_element_type=jnp.float32)
    cotan_gram = lax.psum_scatter(partial_gram, "fsdp", scatter_dimension=0, tiled=True)[0]
    input_gram = lax.dot_general(
        activations, activations, (((1,), (1,)), ((), ())), preferred_element_type=jnp.float32
    )
    labels = group_ids[0]
    same = labels[:, None] == labels[None, :]
    row_terms = jnp.sum(jnp.where(same, input_gram * cotan_gram, 0.0), axis=1)
    squared = jnp.sum(jnp.where(same, row_terms[None, :], 0.0), axis=1)
    factor = clip / jnp.maximum(jnp.sqrt(squared), clip)
    scaled = (activations.astype(jnp.float32) * factor[:, None]).astype(jnp.bfloat16)
    gradient = lax.dot_general(
        cotangents,
        lax.all_gather(scaled, "fsdp", axis=0, tiled=True),
        (((0,), (0,)), ((), ())),
        preferred_element_type=jnp.float32,
    )
    lags = (step_value - slot_ids - 1) % BAND + 1
    columns = jnp.arange(BAND, dtype=jnp.int32)
    lag_weight = jnp.sum(
        jnp.where(columns[None, :] == lags[:, None], band_coefs[None, :], 0.0), axis=1
    )
    history_part = jnp.zeros(history.shape[1:], jnp.float32)
    for position in range(history.shape[0]):
        history_part = history_part + lag_weight[position] * history[position].astype(jnp.float32)
    noise_scale = noise_mult[0] * clip
    combined = lax.psum_scatter(
        gradient + noise_scale * history_part, "dp", scatter_dimension=1, tiled=True
    )
    examples = EX_DEV * lax.axis_size("dp") * lax.axis_size("fsdp")
    noisy_mean = (
        combined + noise_scale * band_coefs[0] * fresh_noise.astype(jnp.float32)
    ) / examples
    new_first = 0.9 * first_moment + 0.1 * noisy_mean
    new_second = 0.999 * second_moment + 0.001 * noisy_mean * noisy_mean
    step_float = step_value.astype(jnp.float32)
    corrected_first = new_first / (1.0 - jnp.power(jnp.float32(0.9), step_float))
    corrected_second = new_second / (1.0 - jnp.power(jnp.float32(0.999), step_float))
    new_weights = weights - 0.002 * corrected_first / (jnp.sqrt(corrected_second) + 1e-08)
    gathered_weights = lax.all_gather(new_weights, "dp", axis=1, tiled=True)
    return (new_weights, new_first, new_second, noisy_mean, gathered_weights, new_history)


def solution(mesh):
    in_specs = (
        P(("dp", "fsdp"), None),
        P("dp", "fsdp"),
        P(("dp", "fsdp"), None),
        P("fsdp", "dp"),
        P("fsdp", "dp"),
        P("fsdp", "dp"),
        P("fsdp", "dp"),
        P("dp", "fsdp", None),
        P("dp"),
        P(),
        P(),
        P(),
    )
    out_specs = (
        P("fsdp", "dp"),
        P("fsdp", "dp"),
        P("fsdp", "dp"),
        P("fsdp", "dp"),
        P("fsdp", None),
        P("dp", "fsdp", None),
    )
    return jax.shard_map(body, mesh=mesh, in_specs=in_specs, out_specs=out_specs, check_vma=False)
```

profile of v0, /device:TPU:0, one launch (start us, length us, event | category | flops | bytes accessed | tf_op | source)
XLA Modules:
  0.0 505.7 jit_solution(12465230712963849113)
XLA Ops:
  7.2 1.5 copy-done
  8.8 1.7 fusion.8
  10.5 0.0 all-gather.4.cloned.1.call-start
  10.6 30.3 %reduce-scatter.3.cloned.1.call-done = f32[1,256,256]{2,1,0:T(8,128)} async-done(((f32[4,256,256]{2,1,0:T(8,128)}), f32[1,256,256]{2,1,0:T(8,128)}) %reduce-scatter.3.cloned.1.call-update) | async-done | bytes 262160 | tf_op jit(solution)/shard_map/reduce_scatter | solution.py:40
  40.9 3.2 fusion.1
  44.1 0.2 fusion.2
  44.3 1.9 multiply_convert_fusion
  46.2 0.0 reduce-scatter.5.cloned.1.call-start
  46.9 12.1 %fusion.6 = (bf16[1,1024,4096]{2,1,0:T(8,128)(2,1)}, bf16[1,1024,4096]{2,1,0:T(8,128)(2,1)}) fusion(bf16[2,1024,4096]{2,1,0:T(8,128)(2,1)} %param.19), kind=kLoop, calls=%fused_computation.22 | loop fusion | bytes 33554432 | tf_op jit(solution)/shard_map/slice | solution.py:63
  59.1 11.9 %copy.41 = bf16[1,1024,4096]{1,2,0:T(8,128)(2,1)} copy(bf16[1,1024,4096]{2,1,0:T(8,128)(2,1)} %get-tuple-element.22) | data formatting | bytes 16777216
  71.0 12.0 %copy.40 = bf16[1,1024,4096]{1,2,0:T(8,128)(2,1)} copy(bf16[1,1024,4096]{2,1,0:T(8,128)(2,1)} %get-tuple-element.21) | data formatting | bytes 16777216
  83.7 0.2 fusion.3
  83.9 0.6 fusion.7
  84.5 110.1 %all-gather.4.cloned.1.call-done = bf16[1024,4096]{1,0:T(8,128)(2,1)} async-done(((bf16[256,4096]{1,0:T(8,128)(2,1)}), bf16[1024,4096]{1,0:T(8,128)(2,1)}) %all-gather.4.cloned.1.call-update) | async-done | bytes 8388624 | tf_op jit(solution)/shard_map/all_gather | solution.py:52
  194.5 22.8 %bitcast_add_fusion = f32[1024,4096]{0,1:T(8,128)} fusion(bf16[1,1024,4096]{1,2,0:T(8,128)(2,1)} %copy.41, bf16[1,1024,4096]{1,2,0:T(8,128)(2,1)} %copy.40, bf16[1024,4096]{1,0:T(8,128)(2,1)} %all-gather.4.cloned.1.call-done, bf16[1024,1024]{1,0:T(8,128)(2,1)S(1)} %copy-done, f32[]{:T(128)} %bitcast.7, f32[]{:T(128)} %bitcast.6, f32[]{:T(128)} %bitcast.4), kind=kOutput, calls=%fused_computation | convolution fusion | flops 8619294720 | bytes 44040204 | tf_op jit(solution)/shard_map/dot_general | solution.py:50
  217.4 0.5 all-gather.8.cloned.1.call-update
  217.9 0.2 all-gather.6.cloned.1.call-start
  218.1 0.4 copy-done.4
  218.5 1.3 copy.32
  219.8 2.3 copy.34
  222.2 3.1 copy.29
  225.3 3.3 copy.33
  228.6 103.2 %reduce-scatter.5.cloned.1.call-done = f32[1024,512]{0,1:T(8,128)} async-done(((f32[1024,4096]{0,1:T(8,128)}), f32[1024,512]{0,1:T(8,128)}) %reduce-scatter.5.cloned.1.call-update) | async-done | bytes 2097168 | tf_op jit(solution)/shard_map/reduce_scatter | solution.py:65
  331.9 7.7 %divide_subtract_fusion = (f32[1024,512]{0,1:T(8,128)}, f32[1024,512]{0,1:T(8,128)}, f32[1024,512]{0,1:T(8,128)}, f32[1024,512]{0,1:T(8,128)}) fusion(f32[1024,512]{0,1:T(8,128)S(1)} %copy.34, f32[]{:T(128)S(6)} %sub.22, f32[]{:T(128)S(6)} %sub.21, f32[1024,512]{0,1:T(8,128)} %reduce-scatter.5.cloned.1.call-done, bf16[1024,512]{0,1:T(8,128)(2,1)S(1)} %copy-done.5, ...), kind=kLoop, calls=%fused_computation.3 | loop fusion | flops 8912896 | bytes 17825804 | tf_op jit(solution)/shard_map/sub | solution.py:77
  339.6 49.8 %all-gather.8.cloned.1.call-done = bf16[1024,4096]{1,0:T(8,128)(2,1)} async-done(((bf16[1024,512]{1,0:T(8,128)(2,1)}), bf16[1024,4096]{1,0:T(8,128)(2,1)}) %all-gather.8.cloned.1.call-update) | async-done | bytes 8388624 | tf_op jit(solution)/shard_map/all_gather | solution.py:36
  389.5 16.7 %broadcast_select_fusion = bf16[2,1024,4096]{2,1,0:T(8,128)(2,1)} fusion(bf16[2,1024,4096]{2,1,0:T(8,128)(2,1)} %param.19, pred[2]{0:T(512)(128)(4,1)S(1)} %broadcast_compare_fusion, bf16[1024,4096]{1,0:T(8,128)(2,1)} %all-gather.8.cloned.1.call-done), kind=kLoop, calls=%fused_computation.1 | loop fusion | flops 8388608 | bytes 41943040 | tf_op jit(solution)/shard_map/jit(_where)/select_n | solution.py:37
  406.2 1.8 copy.35
  408.0 2.9 copy.36
  410.9 3.0 copy.37
  413.9 1.8 copy.38
  415.7 65.8 %all-gather.6.cloned.1.call-done = f32[1024,4096]{0,1:T(8,128)} async-done(((f32[1024,512]{0,1:T(8,128)}), f32[1024,4096]{0,1:T(8,128)}) %all-gather.6.cloned.1.call-update) | async-done | bytes 16777232 | tf_op jit(solution)/shard_map/all_gather | solution.py:78
  481.6 17.6 %copy.39 = f32[1024,4096]{1,0:T(8,128)} copy(f32[1024,4096]{0,1:T(8,128)} %all-gather.6.cloned.1.call-done) | data formatting | bytes 33554432
  (27 shorter events, 0.2 us)
Async XLA Ops:
  7.2 1.6 copy-start
  7.2 33.7 %reduce-scatter.3.cloned.1.call-start = ((), (), s32[]{:S(2)}) async-start(), calls=%async_computation.2 | async-start | bytes 1310720 | tf_op jit(solution)/shard_map/reduce_scatter | solution.py:40
  8.8 32.1 %copy-start.7 = (s32[1,256]{1,0:T(1,128)S(1)}, s32[1,256]{1,0:T(1,128)}, u32[]{:S(2)}) copy-start(s32[1,256]{1,0:T(1,128)} %param.14) | copy-start | bytes 3076
  10.5 184.0 %all-gather.4.cloned.1.call-start = ((), (), s32[]{:S(2)}) async-start(), calls=%async_computation.3 | async-start | bytes 10485760 | tf_op jit(solution)/shard_map/all_gather | solution.py:52
  40.9 3.4 copy-start.6
  46.2 285.6 %reduce-scatter.5.cloned.1.call-start = ((), (), s32[]{:S(2)}) async-start(), calls=%async_computation.4 | async-start | bytes 18874368 | tf_op jit(solution)/shard_map/reduce_scatter | solution.py:65
  71.0 12.6 %copy-start.9 = (s32[2]{0:T(128)S(1)}, s32[2]{0:T(128)}, u32[]{:S(2)}) copy-start(s32[2]{0:T(128)} %param.20) | copy-start | bytes 28
  71.0 12.7 %copy-start.8 = (f32[16]{0:T(128)S(1)}, f32[16]{0:T(128)}, u32[]{:S(2)}) copy-start(f32[16]{0:T(128)} %param.21) | copy-start | bytes 196
  217.3 1.2 copy-start.4
  217.3 172.2 %all-gather.8.cloned.1.call-start = ((), (), s32[]{:S(2)}) async-start(), calls=%async_computation.6 | async-start | bytes 9437184 | tf_op jit(solution)/shard_map/all_gather | solution.py:36
  217.9 263.7 %all-gather.6.cloned.1.call-start = ((), (), s32[]{:S(2)}) async-start(), calls=%async_computation.5 | async-start | bytes 18874368 | tf_op jit(solution)/shard_map/all_gather | solution.py:78
  225.3 106.6 %copy-start.5 = (bf16[1024,512]{0,1:T(8,128)(2,1)S(1)}, bf16[1024,512]{0,1:T(8,128)(2,1)}, u32[]{:S(2)}) copy-start(bf16[1024,512]{0,1:T(8,128)(2,1)} %copy.32) | copy-start | bytes 3145732
  339.6 66.6 %copy-start.2 = (f32[1024,512]{0,1:T(8,128)S(1)}, f32[1024,512]{0,1:T(8,128)}, u32[]{:S(2)}) copy-start(f32[1024,512]{0,1:T(8,128)} %get-tuple-element.18) | copy-start | bytes 6291460
  410.9 3.0 copy-start.3
  481.6 17.6 %copy-start.1 = (bf16[1024,1024]{1,0:T(8,128)(2,1)S(1)}, bf16[1024,1024]{1,0:T(8,128)(2,1)}, u32[]{:S(2)}) copy-start(bf16[1024,1024]{1,0:T(8,128)(2,1)} %param.13) | copy-start | bytes 6291460
Sparse Core Ops, SparseCore 0:
  10.9 29.9 reduce-scatter.2
  46.4 148.1 all-gather.3
  217.4 114.3 reduce-scatter.4
  333.6 55.8 all-gather.7
  391.8 89.7 all-gather.5
where the time goes:
time: 507 us; the launch traced here: 506 us
  waiting for transfers between devices  360 us (71%)
  local copies, waits for them, and re-layouts  75.7 us (15%)
  matrix products  27.7 us (5%)
  other arithmetic  26.8 us (5%)
  between operations  15.3 us (3%)
    all_gather x1, waiting for transfers between devices, body(): lax.all_gather(scaled, 'fsdp', axis=0, tiled=True)  110 us
    reduce_scatter x1, waiting for transfers between devices, body(): lax.psum_scatter(gradient + noise_scale * history_part, 'dp', scatter_dim...  103 us
    all_gather x1, waiting for transfers between devices, body(): gathered_weights = lax.all_gather(new_weights, 'dp', axis=1, tiled=True)  65.8 us
    unnamed x31, local copies, waits for them, and re-layouts  62.9 us
    all_gather x1, waiting for transfers between devices, body(): full_fresh = lax.all_gather(fresh_noise, 'dp', axis=1, tiled=True)  49.8 us
    reduce_scatter x1, waiting for transfers between devices, body(): lax.psum_scatter(partial_gram, 'fsdp', scatter_dimension=0, tiled=True)[0]  30.3 us
    dot_general x1, matrix products, body(): lax.dot_general(cotangents, lax.all_gather(scaled, 'fsdp', axis=0, tiled=...  22.8 us
    select_n x1, other arithmetic, body(): jnp.where((slot_ids == target)[:, None, None], full_fresh[None], history)  16.7 us
  transfers between devices with their start and end apart: 5, of which 5 were waited for; matrix products, arithmetic and copies ran while one was open for 16% of the time, Pallas kernels for 0%

commit v1 on v0

--- a/solution.py
+++ b/solution.py
@@ -75,7 +75,18 @@
     corrected_first = new_first / (1.0 - jnp.power(jnp.float32(0.9), step_float))
     corrected_second = new_second / (1.0 - jnp.power(jnp.float32(0.999), step_float))
     new_weights = weights - 0.002 * corrected_first / (jnp.sqrt(corrected_second) + 1e-08)
-    gathered_weights = lax.all_gather(new_weights, "dp", axis=1, tiled=True)
+    ways = lax.axis_size("dp")
+    up = [(d, (d + 1) % ways) for d in range(ways)]
+    down = [(d, (d - 1) % ways) for d in range(ways)]
+    earlier, later = ([new_weights], [new_weights])
+    for _ in range(ways // 2):
+        earlier.append(lax.ppermute(earlier[-1], "dp", up))
+    for _ in range((ways - 1) // 2):
+        later.append(lax.ppermute(later[-1], "dp", down))
+    line = jnp.concatenate([*earlier[::-1], *later[1:]], axis=1)
+    gathered_weights = jnp.roll(
+        line, (lax.axis_index("dp") - ways // 2) * new_weights.shape[1], axis=1
+    )
     return (new_weights, new_first, new_second, noisy_mean, gathered_weights, new_history)
 
 

time: 507 us -> 594 us (1.17)
  waiting for transfers between devices: 360 us -> 413 us
  local copies, waits for them, and re-layouts: 75.7 us -> 103 us
  starting transfers between devices: 0.38 us -> 8.32 us
    ppermute x0 -> x7, waiting for transfers between devices: none -> 167 us  [the longest x4 167 us: body(): earlier.append(lax.ppermute(earlier[-1], 'dp', up))]
    all_gather x1 -> x0, waiting for transfers between devices: 65.8 us -> none  [body(): gathered_weights = lax.all_gather(new_weights, 'dp', axis=1, tiled=True)]
    all_gather x1, waiting for transfers between devices: 49.8 us -> 0.01 us  [body(): full_fresh = lax.all_gather(fresh_noise, 'dp', axis=1, tiled=True)]
    unnamed x31 -> x50, local copies, waits for them, and re-layouts: 62.9 us -> 82.1 us
    ppermute x0 -> x7, starting transfers between devices: none -> 7.97 us  [the longest x3 7.41 us: body(): later.append(lax.ppermute(later[-1], 'dp', down))]
    dynamic_slice x0 -> x1, local copies, waits for them, and re-layouts: none -> 6.08 us  [body(): jnp.roll(line, (lax.axis_index('dp') - ways // 2) * new_weights.shape[1],...]
  transfers between devices with their start and end apart: 5 -> 11, of which waited for: 5 -> 7; matrix products, arithmetic and copies ran while one was open for 16% -> 15% of each run, Pallas kernels for 0% -> 0%
where the time goes in v1:
time: 594 us; the launch traced here: 593 us
  waiting for transfers between devices  413 us (70%)
  local copies, waits for them, and re-layouts  103 us (17%)
  matrix products  27.7 us (5%)
  other arithmetic  25.6 us (4%)
  between operations  15.4 us (3%)
  starting transfers between devices  8.32 us (1%)
    ppermute x4, waiting for transfers between devices, body(): earlier.append(lax.ppermute(earlier[-1], 'dp', up))  167 us
    all_gather x1, waiting for transfers between devices, body(): lax.all_gather(scaled, 'fsdp', axis=0, tiled=True)  110 us
    reduce_scatter x1, waiting for transfers between devices, body(): lax.psum_scatter(gradient + noise_scale * history_part, 'dp', scatter_dim...  105 us
    unnamed x50, local copies, waits for them, and re-layouts  82.1 us
    reduce_scatter x1, waiting for transfers between devices, body(): lax.psum_scatter(partial_gram, 'fsdp', scatter_dimension=0, tiled=True)[0]  30.4 us
    dot_general x1, matrix products, body(): lax.dot_general(cotangents, lax.all_gather(scaled, 'fsdp', axis=0, tiled=...  22.8 us
    select_n x1, other arithmetic, body(): jnp.where((slot_ids == target)[:, None, None], full_fresh[None], history)  15.6 us
    slice x1, local copies, waits for them, and re-layouts, body(): history[position].astype(jnp.float32)  12.1 us
  transfers between devices with their start and end apart: 11, of which 7 were waited for; matrix products, arithmetic and copies ran while one was open for 15% of the time, Pallas kernels for 0%

profile of v1, /device:TPU:0, one launch (start us, length us, event | category | flops | bytes accessed | tf_op | source)
XLA Modules:
  0.0 593.1 jit_solution(18271576591954307659)
XLA Ops:
  10.6 30.4 %reduce-scatter.3.cloned.1.call-done = f32[1,256,256]{2,1,0:T(8,128)} async-done(((f32[4,256,256]{2,1,0:T(8,128)}), f32[1,256,256]{2,1,0:T(8,128)}) %reduce-scatter.3.cloned.1.call-update) | async-done | bytes 262160 | tf_op jit(solution)/shard_map/reduce_scatter | solution.py:40
  40.9 3.2 fusion.1
  44.3 1.9 multiply_convert_fusion
  47.0 12.1 %fusion.6 = (bf16[1,1024,4096]{2,1,0:T(8,128)(2,1)}, bf16[1,1024,4096]{2,1,0:T(8,128)(2,1)}) fusion(bf16[2,1024,4096]{2,1,0:T(8,128)(2,1)} %param.19), kind=kLoop, calls=%fused_computation.39 | loop fusion | bytes 33554432 | tf_op jit(solution)/shard_map/slice | solution.py:63
  59.1 12.0 %copy.40 = bf16[1,1024,4096]{1,2,0:T(8,128)(2,1)} copy(bf16[1,1024,4096]{2,1,0:T(8,128)(2,1)} %get-tuple-element.21) | data formatting | bytes 16777216
  71.1 12.0 %copy.41 = bf16[1,1024,4096]{1,2,0:T(8,128)(2,1)} copy(bf16[1,1024,4096]{2,1,0:T(8,128)(2,1)} %get-tuple-element.22) | data formatting | bytes 16777216
  84.5 110.0 %all-gather.3.cloned.1.call-done = bf16[1024,4096]{1,0:T(8,128)(2,1)} async-done(((bf16[256,4096]{1,0:T(8,128)(2,1)}), bf16[1024,4096]{1,0:T(8,128)(2,1)}) %all-gather.3.cloned.1.call-update) | async-done | bytes 8388624 | tf_op jit(solution)/shard_map/all_gather | solution.py:52
  194.5 22.8 %bitcast_add_fusion = f32[1024,4096]{0,1:T(8,128)} fusion(bf16[1,1024,4096]{1,2,0:T(8,128)(2,1)} %copy.41, bf16[1,1024,4096]{1,2,0:T(8,128)(2,1)} %copy.40, bf16[1024,4096]{1,0:T(8,128)(2,1)} %all-gather.3.cloned.1.call-done, bf16[1024,1024]{1,0:T(8,128)(2,1)S(1)} %copy-done, f32[]{:T(128)} %bitcast.7, f32[]{:T(128)} %bitcast.6, f32[]{:T(128)} %bitcast.4), kind=kOutput, calls=%fused_computation | convolution fusion | flops 8619294720 | bytes 44040204 | tf_op jit(solution)/shard_map/dot_general | solution.py:50
  220.0 1.8 copy.29
  221.8 3.0 copy.33
  224.8 1.8 copy.34
  226.6 105.2 %reduce-scatter.5.cloned.1.call-done = f32[1024,512]{0,1:T(8,128)} async-done(((f32[1024,4096]{0,1:T(8,128)}), f32[1024,512]{0,1:T(8,128)}) %reduce-scatter.5.cloned.1.call-update) | async-done | bytes 2097168 | tf_op jit(solution)/shard_map/reduce_scatter | solution.py:65
  331.9 7.6 %divide_subtract_fusion = (f32[1024,512]{0,1:T(8,128)S(1)}, f32[1024,512]{0,1:T(8,128)}, f32[1024,512]{0,1:T(8,128)}, f32[1024,512]{0,1:T(8,128)}) fusion(f32[1024,512]{0,1:T(8,128)} %copy.34, f32[]{:T(128)S(6)} %sub.29, f32[]{:T(128)S(6)} %sub.28, f32[1024,512]{0,1:T(8,128)} %reduce-scatter.5.cloned.1.call-done, bf16[1024,512]{0,1:T(8,128)(2,1)S(1)} %copy-done.5, ...), kind=kLoop, calls=%fused_computation.3 | loop fusion | flops 8912896 | bytes 17825804 | tf_op jit(solution)/shard_map/sub | solution.py:77
  339.5 52.6 %collective-permute-done = f32[1024,512]{0,1:T(8,128)S(1)} collective-permute-done((f32[1024,512]{0,1:T(8,128)S(1)}, f32[1024,512]{0,1:T(8,128)S(1)}, u32[]{:S(2)}, u32[]{:S(2)}) %collective-permute-start) | collective-permute-done | bytes 2097184 | tf_op jit(solution)/shard_map/ppermute | solution.py:83
  392.7 2.1 collective-permute-start.4
  394.8 49.8 %collective-permute-done.1 = f32[1024,512]{0,1:T(8,128)} collective-permute-done((f32[1024,512]{0,1:T(8,128)S(1)}, f32[1024,512]{0,1:T(8,128)}, u32[]{:S(2)}, u32[]{:S(2)}) %collective-permute-start.1) | collective-permute-done | bytes 2097184 | tf_op jit(solution)/shard_map/ppermute | solution.py:83
  444.6 2.6 collective-permute-start.5
  447.3 45.9 %collective-permute-done.2 = f32[1024,512]{0,1:T(8,128)} collective-permute-done((f32[1024,512]{0,1:T(8,128)}, f32[1024,512]{0,1:T(8,128)}, u32[]{:S(2)}, u32[]{:S(2)}) %collective-permute-start.2) | collective-permute-done | bytes 2097184 | tf_op jit(solution)/shard_map/ppermute | solution.py:83
  493.2 2.7 collective-permute-start.6
  495.9 15.6 %broadcast_select_fusion = bf16[2,1024,4096]{2,1,0:T(8,128)(2,1)} fusion(bf16[2,1024,4096]{2,1,0:T(8,128)(2,1)} %param.19, pred[2]{0:T(512)(128)(4,1)S(1)} %broadcast_compare_fusion, bf16[1024,4096]{1,0:T(8,128)(2,1)} %all-gather.5.cloned.1.call-done), kind=kLoop, calls=%fused_computation.1 | loop fusion | flops 8388608 | bytes 41943040 | tf_op jit(solution)/shard_map/jit(_where)/select_n | solution.py:37
  511.5 1.8 copy.35
  513.3 2.9 copy.36
  516.2 2.9 copy.37
  519.1 2.9 copy.38
  521.9 19.1 %collective-permute-done.3 = f32[1024,512]{0,1:T(8,128)} collective-permute-done((f32[1024,512]{0,1:T(8,128)}, f32[1024,512]{0,1:T(8,128)}, u32[]{:S(2)}, u32[]{:S(2)}) %collective-permute-start.3) | collective-permute-done | bytes 2097184 | tf_op jit(solution)/shard_map/ppermute | solution.py:83
  542.8 1.9 constant_dynamic-update-slice_fusion.14
  552.1 1.7 constant_dynamic-update-slice_fusion.7
  555.5 1.7 constant_dynamic-update-slice_fusion.5
  557.7 1.7 constant_dynamic-update-slice_fusion.2
  561.1 1.7 constant_dynamic-update-slice_fusion
  562.9 6.1 %constant_dynamic-slice_fusion = f32[1024,4096]{0,1:T(8,128)} fusion(f32[1024,8192]{0,1:T(8,128)S(1)} %constant_dynamic-update-slice_fusion, s32[]{:T(128)S(6)} %select_n.46), kind=kLoop, calls=%fused_computation.38 | loop fusion | bytes 33554436 | tf_op jit(solution)/shard_map/jit(_roll_dynamic)/dynamic_slice | solution.py:87
  569.0 17.6 %copy.39 = f32[1024,4096]{1,0:T(8,128)} copy(f32[1024,4096]{0,1:T(8,128)} %constant_dynamic-slice_fusion) | data formatting | bytes 33554432
  (59 shorter events, 20.4 us)
Async XLA Ops:
  7.2 1.6 copy-start
  7.2 33.7 %copy-start.9 = (s32[1,256]{1,0:T(1,128)S(1)}, s32[1,256]{1,0:T(1,128)}, u32[]{:S(2)}) copy-start(s32[1,256]{1,0:T(1,128)} %param.14) | copy-start | bytes 3076
  7.2 33.7 %reduce-scatter.3.cloned.1.call-start = ((), (), s32[]{:S(2)}) async-start(), calls=%async_computation.2 | async-start | bytes 1310720 | tf_op jit(solution)/shard_map/reduce_scatter | solution.py:40
  10.5 184.0 %all-gather.3.cloned.1.call-start = ((), (), s32[]{:S(2)}) async-start(), calls=%async_computation.3 | async-start | bytes 10485760 | tf_op jit(solution)/shard_map/all_gather | solution.py:52
  40.9 3.4 copy-start.6
  46.3 285.6 %reduce-scatter.5.cloned.1.call-start = ((), (), s32[]{:S(2)}) async-start(), calls=%async_computation.4 | async-start | bytes 18874368 | tf_op jit(solution)/shard_map/reduce_scatter | solution.py:65
  71.1 12.6 %copy-start.11 = (s32[2]{0:T(128)S(1)}, s32[2]{0:T(128)}, u32[]{:S(2)}) copy-start(s32[2]{0:T(128)} %param.20) | copy-start | bytes 28
  71.1 12.7 %copy-start.10 = (f32[16]{0:T(128)S(1)}, f32[16]{0:T(128)}, u32[]{:S(2)}) copy-start(f32[16]{0:T(128)} %param.21) | copy-start | bytes 196
  217.3 1.2 copy-start.4
  217.3 2.6 copy-start.7
  217.3 278.5 %all-gather.5.cloned.1.call-start = ((), (), s32[]{:S(2)}) async-start(), calls=%async_computation.5 | async-start | bytes 9437184 | tf_op jit(solution)/shard_map/all_gather | solution.py:36
  221.8 3.0 copy-start.8
  221.8 110.1 %copy-start.5 = (bf16[1024,512]{0,1:T(8,128)(2,1)S(1)}, bf16[1024,512]{0,1:T(8,128)(2,1)}, u32[]{:S(2)}) copy-start(bf16[1024,512]{0,1:T(8,128)(2,1)} %copy.32) | copy-start | bytes 3145732
  339.5 52.6 %collective-permute-start = (f32[1024,512]{0,1:T(8,128)S(1)}, f32[1024,512]{0,1:T(8,128)S(1)}, u32[]{:S(2)}, u32[]{:S(2)}) collective-permute-start(f32[1024,512]{0,1:T(8,128)S(1)} %get-tuple-element.18), channel_id=1, source_target_pairs={{0,4},{4,8},{8,12},{12,16},{16,20},{20,24},{24,28},{28,0},{1,5},{5... | collective-permute-start | bytes 6291464 | tf_op jit(solution)/shard_map/ppermute | solution.py:83
  392.2 52.5 %copy-start.2 = (f32[1024,512]{0,1:T(8,128)}, f32[1024,512]{0,1:T(8,128)S(1)}, u32[]{:S(2)}) copy-start(f32[1024,512]{0,1:T(8,128)S(1)} %collective-permute-done) | copy-start | bytes 6291460
  392.2 52.5 %collective-permute-start.1 = (f32[1024,512]{0,1:T(8,128)S(1)}, f32[1024,512]{0,1:T(8,128)}, u32[]{:S(2)}, u32[]{:S(2)}) collective-permute-start(f32[1024,512]{0,1:T(8,128)S(1)} %collective-permute-done), channel_id=1, source_target_pairs={{0,4},{4,8},{8,12},{12,16},{16,20},{20,24},{24,28},{28,0},{1,5},{5... | collective-permute-start | bytes 6291464 | tf_op jit(solution)/shard_map/ppermute | solution.py:83
  392.7 51.9 %collective-permute-start.4 = (f32[1024,512]{0,1:T(8,128)S(1)}, f32[1024,512]{0,1:T(8,128)}, u32[]{:S(2)}, u32[]{:S(2)}) collective-permute-start(f32[1024,512]{0,1:T(8,128)S(1)} %get-tuple-element.18), channel_id=1, source_target_pairs={{0,28},{4,0},{8,4},{12,8},{16,12},{20,16},{24,20},{28,24},{1,29},{... | collective-permute-start | bytes 6291464 | tf_op jit(solution)/shard_map/ppermute | solution.py:85
  444.6 48.5 %collective-permute-start.2 = (f32[1024,512]{0,1:T(8,128)}, f32[1024,512]{0,1:T(8,128)}, u32[]{:S(2)}, u32[]{:S(2)}) collective-permute-start(f32[1024,512]{0,1:T(8,128)} %collective-permute-done.1), channel_id=1, source_target_pairs={{0,4},{4,8},{8,12},{12,16},{16,20},{20,24},{24,28},{28,0},{1,5},{5... | collective-permute-start | bytes 6291464 | tf_op jit(solution)/shard_map/ppermute | solution.py:83
  444.6 48.5 %collective-permute-start.5 = (f32[1024,512]{0,1:T(8,128)}, f32[1024,512]{0,1:T(8,128)}, u32[]{:S(2)}, u32[]{:S(2)}) collective-permute-start(f32[1024,512]{0,1:T(8,128)} %collective-permute-done.4), channel_id=1, source_target_pairs={{0,28},{4,0},{8,4},{12,8},{16,12},{20,16},{24,20},{28,24},{1,29},{... | collective-permute-start | bytes 6291464 | tf_op jit(solution)/shard_map/ppermute | solution.py:85
  493.2 47.9 %collective-permute-start.3 = (f32[1024,512]{0,1:T(8,128)}, f32[1024,512]{0,1:T(8,128)}, u32[]{:S(2)}, u32[]{:S(2)}) collective-permute-start(f32[1024,512]{0,1:T(8,128)} %collective-permute-done.2), channel_id=1, source_target_pairs={{0,4},{4,8},{8,12},{12,16},{16,20},{20,24},{24,28},{28,0},{1,5},{5... | collective-permute-start | bytes 6291464 | tf_op jit(solution)/shard_map/ppermute | solution.py:83
  493.2 57.1 %collective-permute-start.6 = (f32[1024,512]{0,1:T(8,128)}, f32[1024,512]{0,1:T(8,128)}, u32[]{:S(2)}, u32[]{:S(2)}) collective-permute-start(f32[1024,512]{0,1:T(8,128)} %collective-permute-done.5), channel_id=1, source_target_pairs={{0,28},{4,0},{8,4},{12,8},{16,12},{20,16},{24,20},{28,24},{1,29},{... | collective-permute-start | bytes 6291464 | tf_op jit(solution)/shard_map/ppermute | solution.py:85
  542.8 3.6 copy-start.3
  568.9 17.6 %copy-start.1 = (bf16[1024,1024]{1,0:T(8,128)(2,1)S(1)}, bf16[1024,1024]{1,0:T(8,128)(2,1)}, u32[]{:S(2)}) copy-start(bf16[1024,1024]{1,0:T(8,128)(2,1)} %param.13) | copy-start | bytes 6291460
Sparse Core Ops, SparseCore 0:
  10.9 29.9 reduce-scatter.2
  46.4 148.1 all-gather.2
  217.4 114.3 reduce-scatter.4
  333.6 70.7 all-gather.4
